TPU v7x, 32 devices: a whole 2x2x4 slice. The times are simulated.
32 devices in a mesh: gx: 8 (over z, x), gy: 4 (over y, core).
Axes of the slice: x: 2, y: 2, z: 4, core: 2. Of those that a mesh axis runs over, the one named last changes fastest.
Arguments:
- fields: bfloat16 [4, 64, 128, 256], P(None, 'gx', 'gy'), may hold values from -6 to 6
- rows_live: int32 [8], replicated, may hold values from 4 to 8, as said below
- cols_live: int32 [4], replicated, may hold values from 16 to 32, as said below
- weight: bfloat16 [32, 108], replicated, may hold values from -0.625 to 0.625
- bias: float32 [32], replicated, may hold values from -3 to 3
- grad_out: bfloat16 [32, 32, 64, 128], P('gy', 'gx'), may hold values from -0.0625 to 0.0625
Outputs:
- stem: bfloat16 [32, 32, 64, 128], P('gy', 'gx')
- weight_grad: float32 [32, 108], P('gy')
- bias_grad: float32 [32], P('gy')
Inputs may be any that keep to these rules, and one draw needn't show every extreme that they name: `rows_live`: every entry is even, and some entry equals 8. `cols_live`: every entry is even, and some entry equals 32.
All inputs are finite; a program needn't handle non-finite values.
Results may differ from a plain program's by a relative error of at most 0.0054.
Values may be sent and summed in bfloat16 or wider, within the bound.
No kernel may reach another device: no remote copies, remote signals or barrier semaphores. Data moves between devices by JAX's collectives and lax.ppermute only.
A program may use at most 64 MiB of HBM per device.

v0:
```python
import jax
import jax.numpy as jnp
from jax import lax
from jax.sharding import PartitionSpec as P


def from_behind(block, axis, distance):
    devices = range(lax.axis_size(axis))
    route = [(i - distance, i) for i in devices if i - distance in devices]
    return lax.ppermute(block, axis, route)


def extend(data, border, count, dim):
    length = data.shape[dim]
    border_wide = jnp.expand_dims(border, dim)
    joined = jnp.concatenate([jnp.zeros_like(border_wide), data], axis=dim)
    shape = [1] * joined.ndim
    shape[dim] = length + 1
    places = jnp.arange(length + 1, dtype=jnp.int32).reshape(shape)
    edge_at = length - count
    kept = jnp.where(places > edge_at, joined, jnp.zeros_like(joined))
    return jnp.where(places == edge_at, border_wide, kept)


def taps(padded, axes, halves):
    pieces = []
    for off_x in range(3):
        for off_y in range(3):
            for off_z in range(3):
                piece = padded
                for axis_no, offset, half in zip(axes, (off_x, off_y, off_z), halves):
                    piece = lax.slice_in_dim(piece, offset, offset + 2 * half - 1, 2, axis_no)
                pieces.append(piece)
    return pieces


def local(fields, rows_live, cols_live, weight, bias, grad_out):
    in_chans, cap_x, cap_y, depth = fields.shape
    half_x = cap_x // 2
    half_y = cap_y // 2
    half_z = depth // 2
    out_chans = weight.shape[0]
    tiles_y = lax.axis_size("gy")
    row_count = rows_live[lax.axis_index("gx")]
    above = from_behind(fields[:, cap_x - 1], "gx", 1)
    ext_rows = extend(fields, above, row_count, 1)
    row_ok = jnp.arange(half_x, dtype=jnp.int32) >= half_x - row_count // 2
    col_count = cols_live[lax.axis_index("gy")]
    beside = from_behind(ext_rows[:, :, cap_y - 1], "gy", 1)
    ext_full = extend(ext_rows, beside, col_count, 2)
    lhs = ext_full[None]
    kernel = weight.reshape(out_chans, in_chans, 3, 3, 3)
    dims = ("NCDHW", "OIDHW", "NCDHW")
    conv = (
        lax.conv_general_dilated(
            lhs,
            kernel,
            (2, 2, 2),
            ((0, 0), (0, 0), (1, 0)),
            dimension_numbers=dims,
            preferred_element_type=jnp.float32,
        )[0]
        + bias[:, None, None, None]
    )
    col_ok = jnp.arange(half_y, dtype=jnp.int32) >= half_y - col_count // 2
    live = (row_ok[:, None] & col_ok[None, :]).reshape(1, half_x, half_y, 1)
    pre_local = jnp.where(live, conv, 0.0).astype(jnp.bfloat16)
    regrouped = lax.all_to_all(pre_local, "gy", split_axis=0, concat_axis=2, tiled=True)
    pre_wide = regrouped.astype(jnp.float32)
    sigma = jax.nn.sigmoid(pre_wide)
    stem = (pre_wide * sigma).astype(jnp.bfloat16)
    wide_cols = jnp.arange(half_y, dtype=jnp.int32)[None, :] >= half_y - (cols_live // 2)[:, None]
    wide_live = row_ok.reshape(1, half_x, 1, 1) & wide_cols.reshape(1, 1, tiles_y * half_y, 1)
    slope = sigma * (1.0 + pre_wide * (1.0 - sigma))
    grad_pre = jnp.where(wide_live, grad_out.astype(jnp.float32) * slope, 0.0).astype(jnp.bfloat16)
    returned = lax.all_to_all(grad_pre, "gy", split_axis=2, concat_axis=0, tiled=True)
    filt = lax.conv_general_dilated(
        ext_full[:, None],
        returned[:, None],
        (1, 1, 1),
        ((0, 0), (0, 0), (1, 0)),
        rhs_dilation=(2, 2, 2),
        dimension_numbers=dims,
        preferred_element_type=jnp.float32,
    )
    weight_full = jnp.swapaxes(filt, 0, 1).reshape(out_chans, -1)
    bias_full = jnp.sum(returned.astype(jnp.float32), axis=(1, 2, 3))
    packed = jnp.concatenate([weight_full, bias_full[:, None]], axis=1)
    total = lax.psum(packed, ("gx", "gy"))
    rows = out_chans // tiles_y
    mine = lax.dynamic_slice_in_dim(total, lax.axis_index("gy") * rows, rows, 0)
    weight_grad, bias_grad = (mine[:, :-1], mine[:, -1])
    return (stem, weight_grad, bias_grad)


def solution(mesh):
    in_specs = (P(None, "gx", "gy", None), P(), P(), P(), P(), P("gy", "gx", None, None))
    out_specs = (P("gy", "gx", None, None), P("gy", None), P("gy"))
    return jax.shard_map(local, mesh=mesh, in_specs=in_specs, out_specs=out_specs, check_vma=False)
```

profile of v0, /device:TPU:0, one launch (start us, length us, event | category | flops | bytes accessed | tf_op | source)
XLA Modules:
  0.0 264.5 jit_solution(15220797202595424917)
XLA Ops:
  0.6 0.9 slice_bitcast_fusion
  1.5 4.9 %collective-permute-start = (bf16[4,32,256]{2,1,0:T(8,128)(2,1)S(1)}, bf16[4,32,256]{2,1,0:T(8,128)(2,1)S(1)}, u32[]{:S(2)}, u32[]{:S(2)}) collective-permute-start(bf16[4,32,256]{2,1,0:T(8,128)(2,1)S(1)} %slice_bitcast_fusion), channel_id=1, source_target_pairs={{0,4},{4,8},{8,12},{12,16},{16,20},{20,24},{24,28},{1,5},{5,9},{9,... | collective-permute-start | bytes 196616 | tf_op jit(solution)/shard_map/ppermute | solution.py:10
  6.4 1.2 dynamic_slice.10
  10.2 1.2 dynamic_slice.9
  14.7 0.7 fusion.20
  16.1 0.1 broadcast_and_fusion.1
  16.1 1.2 select_select_fusion.1
  17.4 1.5 collective-permute-start.1
  18.9 0.8 copy.105
  19.7 0.7 reshape.142
  20.4 0.0 collective-permute-done.1
  20.4 0.0 copy-start.6
  20.4 1.3 fusion.24
  21.7 0.5 pad.2
  22.2 2.2 reshape.158
  24.4 0.0 copy-start.3
  24.4 12.6 %copy.104 = bf16[4,9,33,1,8,34]{4,0,5,2,1,3:T(4,128)(2,1)} copy(bf16[4,9,33,1,8,34]{5,4,2,1,0,3:T(8,128)(2,1)S(1)} %reshape.158) | data formatting | bytes 1292544 | tf_op jit(solution)/shard_map/conv_general_dilated | solution.py:55
  37.0 1.5 slice.19
  38.5 14.1 %broadcast_select_fusion = f32[4,16,8,17,32]{4,2,3,1,0:T(8,128)S(1)} fusion(pred[8,17]{0,1:T(8,128)(4,1)S(1)} %copy-done.6, bf16[4,9,33,1,7,2]{4,0,5,2,1,3:T(4,128)(2,1)S(1)} %slice.19, bf16[4,9,33,1,8,34]{4,0,5,2,1,3:T(4,128)(2,1)} %copy.104, bf16[32,4,3,3,3]{0,4,3,2,1:T(4,128)(2,1)S(1)} %copy-done.3), kind=kOutput, calls=%fused_computation.6 | convolution fusion | flops 62493440 | bytes 1800696 | tf_op jit(solution)/shard_map/conv_general_dilated | solution.py:55
  52.6 0.0 copy-start.5
  52.6 0.8 copy.107
  53.4 0.0 copy-start.1
  53.4 2.2 slice.20
  55.6 3.5 %copy.121 = f32[4,16,1,128,32]{3,1,0,4,2:T(8,128)S(1)} copy(f32[4,16,1,128,32]{4,1,3,0,2:T(8,128)} %slice.20) | data formatting | bytes 2097152
  59.2 1.1 fusion.9
  60.2 4.9 %all-to-all-start = ((bf16[32,4,16,128]{3,2,1,0:T(8,128)(2,1)}), bf16[32,4,16,128]{3,2,1,0:T(8,128)(2,1)S(1)}, u32[]{:S(2)}, u32[]{:S(2)}) async-start(bf16[32,4,16,128]{3,2,1,0:T(8,128)(2,1)} %fusion.9), calls=%async_computation | async-start | bytes 1048576 | tf_op jit(solution)/shard_map/all_to_all | solution.py:68
  65.1 0.1 iota_compare_fusion.1
  65.2 0.1 ge.51
  65.3 0.1 broadcast_and_fusion
  65.4 8.6 %all-to-all-done = bf16[32,4,16,128]{3,2,1,0:T(8,128)(2,1)S(1)} async-done(((bf16[32,4,16,128]{3,2,1,0:T(8,128)(2,1)}), bf16[32,4,16,128]{3,2,1,0:T(8,128)(2,1)S(1)}, u32[]{:S(2)}, u32[]{:S(2)}) %all-to-all-start) | async-done | bytes 524320 | tf_op jit(solution)/shard_map/all_to_all | solution.py:68
  74.0 0.1 convert_bitcast_fusion
  74.1 0.1 copy.109
  74.2 1.3 fusion.18
  75.5 1.2 copy.110
  76.7 3.6 %all-to-all-start.1 = ((bf16[8,4,64,128]{3,1,0,2:T(4,128)(2,1)}), bf16[8,4,64,128]{3,1,0,2:T(4,128)(2,1)S(1)}, u32[]{:S(2)}, u32[]{:S(2)}) async-start(bf16[8,4,64,128]{3,1,0,2:T(4,128)(2,1)} %copy.110), calls=%async_computation.1 | async-start | bytes 1048576 | tf_op jit(solution)/shard_map/all_to_all | solution.py:76
  80.4 48.7 %copy.113 = bf16[4,1,9,33,256]{0,1,4,3,2:T(2,128)(2,1)} copy(bf16[4,1,9,33,256]{4,3,2,0,1:T(8,128)(2,1)S(1)} %copy-done) | data formatting | bytes 1216512 | tf_op jit(solution)/shard_map/broadcast_in_dim | solution.py:78
  129.1 0.0 all-to-all-done.1
  129.1 0.2 copy.111
  129.3 0.2 convert_reduce_fusion
  129.5 0.1 copy.112
  129.6 0.1 copy.116
  129.7 0.7 broadcast_in_dim.115
  130.4 4.8 %copy.114 = bf16[32,1,4,16,128]{0,1,4,3,2:T(2,128)(2,1)} copy(bf16[32,1,4,16,128]{4,3,2,0,1:T(8,128)(2,1)S(1)} %bitcast.72) | data formatting | bytes 1048576 | tf_op jit(solution)/shard_map/broadcast_in_dim | solution.py:79
  135.1 87.7 %fusion.26 = f32[32,4,3,3,3]{0,1,4,3,2:T(4,128)S(1)} fusion(bf16[4,1,9,33,256]{0,1,4,3,2:T(2,128)(2,1)} %copy.113, bf16[32,1,4,16,128]{0,1,4,3,2:T(2,128)(2,1)} %copy.114), kind=kOutput, calls=%fused_computation.51 | convolution fusion | flops 56475648 | bytes 1146368 | tf_op jit(solution)/shard_map/transpose | solution.py:86
  222.9 0.1 copy.117
  222.9 0.1 pad_maximum_fusion
  223.0 40.8 %psum.7 = f32[32,109]{1,0:T(8,128)S(1)} all-reduce(f32[32,109]{1,0:T(8,128)S(1)} %pad_maximum_fusion), channel_id=1, replica_groups=mesh['gx'=8,'gy'=4] {'gx','gy'}, use_global_device_ids=true, to_apply=%region_1.2 | all-reduce | flops 3488 | bytes 27904 | tf_op jit(solution)/shard_map/psum | solution.py:89
  263.8 0.7 slice_reduce_fusion
  (21 shorter events, 0.2 us)
Async XLA Ops:
  1.5 14.7 %collective-permute-start = (bf16[4,32,256]{2,1,0:T(8,128)(2,1)S(1)}, bf16[4,32,256]{2,1,0:T(8,128)(2,1)S(1)}, u32[]{:S(2)}, u32[]{:S(2)}) collective-permute-start(bf16[4,32,256]{2,1,0:T(8,128)(2,1)S(1)} %slice_bitcast_fusion), channel_id=1, source_target_pairs={{0,4},{4,8},{8,12},{12,16},{16,20},{20,24},{24,28},{1,5},{5,9},{9,... | collective-permute-start | bytes 196616 | tf_op jit(solution)/shard_map/ppermute | solution.py:10
  17.4 3.0 %collective-permute-start.1 = (bf16[4,9,256]{2,0,1:T(4,128)(2,1)S(1)}, bf16[4,9,256]{2,0,1:T(4,128)(2,1)S(1)}, u32[]{:S(2)}, u32[]{:S(2)}) collective-permute-start(bf16[4,9,256]{2,0,1:T(4,128)(2,1)S(1)} %bitcast.73), channel_id=1, source_target_pairs={{0,1},{1,2},{2,3},{4,5},{5,6},{6,7},{8,9},{9,10},{10,11},{12,13},{... | collective-permute-start | bytes 55304 | tf_op jit(solution)/shard_map/ppermute | solution.py:10
  20.4 18.1 %copy-start.6 = (pred[8,17]{0,1:T(8,128)(4,1)S(1)}, pred[8,17]{0,1:T(8,128)(4,1)}, u32[]{:S(2)}) copy-start(pred[8,17]{0,1:T(8,128)(4,1)} %constant.67) | copy-start | bytes 412
  24.4 14.1 %copy-start.3 = (bf16[32,4,3,3,3]{0,4,3,2,1:T(4,128)(2,1)S(1)}, bf16[32,4,3,3,3]{0,4,3,2,1:T(4,128)(2,1)}, u32[]{:S(2)}) copy-start(bf16[32,4,3,3,3]{0,4,3,2,1:T(4,128)(2,1)} %reshape.142) | copy-start | bytes 20740
  52.6 6.6 %copy-start.5 = (f32[32]{0:T(128)S(1)}, f32[32]{0:T(128)}, u32[]{:S(2)}) copy-start(f32[32]{0:T(128)} %param.10) | copy-start | bytes 388
  53.4 20.8 %copy-start.1 = (bf16[8,4,64,128]{3,2,1,0:T(8,128)(2,1)S(1)}, bf16[8,4,64,128]{3,2,1,0:T(8,128)(2,1)}, u32[]{:S(2)}) copy-start(bf16[8,4,64,128]{3,2,1,0:T(8,128)(2,1)} %param.11) | copy-start | bytes 1572868
  53.4 27.0 %copy-start = (bf16[4,1,9,33,256]{4,3,2,0,1:T(8,128)(2,1)S(1)}, bf16[4,1,9,33,256]{4,3,2,0,1:T(8,128)(2,1)}, u32[]{:S(2)}) copy-start(bf16[4,1,9,33,256]{4,3,2,0,1:T(8,128)(2,1)} %get-tuple-element.11) | copy-start | bytes 1824772
  60.2 13.7 %all-to-all-start = ((bf16[32,4,16,128]{3,2,1,0:T(8,128)(2,1)}), bf16[32,4,16,128]{3,2,1,0:T(8,128)(2,1)S(1)}, u32[]{:S(2)}, u32[]{:S(2)}) async-start(bf16[32,4,16,128]{3,2,1,0:T(8,128)(2,1)} %fusion.9), calls=%async_computation | async-start | bytes 1048576 | tf_op jit(solution)/shard_map/all_to_all | solution.py:68
  76.7 52.4 %all-to-all-start.1 = ((bf16[8,4,64,128]{3,1,0,2:T(4,128)(2,1)}), bf16[8,4,64,128]{3,1,0,2:T(4,128)(2,1)S(1)}, u32[]{:S(2)}, u32[]{:S(2)}) async-start(bf16[8,4,64,128]{3,1,0,2:T(4,128)(2,1)} %copy.110), calls=%async_computation.1 | async-start | bytes 1048576 | tf_op jit(solution)/shard_map/all_to_all | solution.py:76
  135.1 87.8 %copy-start.2 = (f32[32,1]{1,0:T(8,128)S(1)}, f32[32,1]{1,0:T(8,128)}, u32[]{:S(2)}) copy-start(f32[32,1]{1,0:T(8,128)} %broadcast_in_dim.115) | copy-start | bytes 388
  263.8 0.7 copy-start.4
where the time goes:
time: 265 us
  matrix products  102 us (38%)
  local copies, waits for them, and re-layouts  84.9 us (32%)
  blocking collectives  40.8 us (15%)
  starting transfers between devices  14.9 us (6%)
  waiting for transfers between devices  8.58 us (3%)
  between operations  7.43 us (3%)
  other arithmetic  6.22 us (2%)
    transpose x1, matrix products, local(): weight_full = jnp.swapaxes(filt, 0, 1).reshape(out_chans, -1)  87.7 us
    broadcast_in_dim x1, local copies, waits for them, and re-layouts, local(): ext_full[:, None]  48.7 us
    psum x1, blocking collectives, local(): total = lax.psum(packed, ('gx', 'gy'))  40.8 us
    conv_general_dilated x5, local copies, waits for them, and re-layouts, local(): lax.conv_general_dilated(lhs, kernel, (2, 2, 2), ((0, 0), (0, 0), (1, 0))...  19.2 us
    conv_general_dilated x1, matrix products, local(): lax.conv_general_dilated(lhs, kernel, (2, 2, 2), ((0, 0), (0, 0), (1, 0))...  14.1 us
    all_to_all x1, waiting for transfers between devices, local(): lax.all_to_all(pre_local, 'gy', split_axis=0, concat_axis=2, tiled=True)  8.57 us
    ppermute x2, starting transfers between devices, from_behind(): return lax.ppermute(block, axis, route)  6.32 us
  transfers between devices with their start and end apart: 4, of which 1 were waited for; matrix products, arithmetic and copies ran while one was open for 20% of the time, Pallas kernels for 0%

commit v1 on v0

--- a/solution.py
+++ b/solution.py
@@ -65,7 +65,9 @@
     col_ok = jnp.arange(half_y, dtype=jnp.int32) >= half_y - col_count // 2
     live = (row_ok[:, None] & col_ok[None, :]).reshape(1, half_x, half_y, 1)
     pre_local = jnp.where(live, conv, 0.0).astype(jnp.bfloat16)
-    regrouped = lax.all_to_all(pre_local, "gy", split_axis=0, concat_axis=2, tiled=True)
+    regrouped = jnp.concatenate(
+        lax.all_to_all(jnp.stack(jnp.split(pre_local, lax.axis_size("gy"), 0), 0), "gy", 0, 0), 2
+    )
     pre_wide = regrouped.astype(jnp.float32)
     sigma = jax.nn.sigmoid(pre_wide)
     stem = (pre_wide * sigma).astype(jnp.bfloat16)

time: 265 us -> 276 us (1.042)
  local copies, waits for them, and re-layouts: 84.9 us -> 94.4 us
    another operation x0 -> x5, local copies, waits for them, and re-layouts: none -> 16.2 us  [local(): jnp.stack(jnp.split(pre_local, lax.axis_size('gy'), 0), 0)]
    unnamed x16 -> x15, local copies, waits for them, and re-layouts: 4.38 us -> 0.85 us
    conv_general_dilated x5 -> x4, local copies, waits for them, and re-layouts: 19.2 us -> 17.1 us  [local(): lax.conv_general_dilated(lhs, kernel, (2, 2, 2), ((0, 0), (0, 0), (1, 0))...]
  transfers between devices with their start and end apart: 4 -> 4, of which waited for: 1 -> 1; matrix products, arithmetic and copies ran while one was open for 20% -> 19% of each run, Pallas kernels for 0% -> 0%
where the time goes in v1:
time: 276 us; the launch traced here: 275 us
  matrix products  102 us (37%)
  local copies, waits for them, and re-layouts  94.4 us (34%)
  blocking collectives  41 us (15%)
  starting transfers between devices  14.7 us (5%)
  waiting for transfers between devices  8.58 us (3%)
  other arithmetic  7.43 us (3%)
  between operations  7.4 us (3%)
    transpose x1, matrix products, local(): weight_full = jnp.swapaxes(filt, 0, 1).reshape(out_chans, -1)  87.7 us
    broadcast_in_dim x1, local copies, waits for them, and re-layouts, local(): ext_full[:, None]  48 us
    psum x1, blocking collectives, local(): total = lax.psum(packed, ('gx', 'gy'))  41 us
    conv_general_dilated x4, local copies, waits for them, and re-layouts, local(): lax.conv_general_dilated(lhs, kernel, (2, 2, 2), ((0, 0), (0, 0), (1, 0))...  17.1 us
    another operation x5, local copies, waits for them, and re-layouts, local(): jnp.stack(jnp.split(pre_local, lax.axis_size('gy'), 0), 0)  16.2 us
    conv_general_dilated x1, matrix products, local(): lax.conv_general_dilated(lhs, kernel, (2, 2, 2), ((0, 0), (0, 0), (1, 0))...  14.1 us
    all_to_all x1, waiting for transfers between devices, local(): lax.all_to_all(jnp.stack(jnp.split(pre_local, lax.axis_size('gy'), 0), 0)...  8.57 us
    ppermute x2, starting transfers between devices, from_behind(): return lax.ppermute(block, axis, route)  6.32 us
  transfers between devices with their start and end apart: 4, of which 1 were waited for; matrix products, arithmetic and copies ran while one was open for 19% of the time, Pallas kernels for 0%

profile of v1, /device:TPU:0, one launch (start us, length us, event | category | flops | bytes accessed | tf_op | source)
XLA Modules:
  0.0 275.3 jit_solution(12574723619589855716)
XLA Ops:
  0.6 0.9 slice_bitcast_fusion.5
  1.5 4.9 %collective-permute-start = (bf16[4,32,256]{2,1,0:T(8,128)(2,1)S(1)}, bf16[4,32,256]{2,1,0:T(8,128)(2,1)S(1)}, u32[]{:S(2)}, u32[]{:S(2)}) collective-permute-start(bf16[4,32,256]{2,1,0:T(8,128)(2,1)S(1)} %slice_bitcast_fusion.5), channel_id=1, source_target_pairs={{0,4},{4,8},{8,12},{12,16},{16,20},{20,24},{24,28},{1,5},{5,9},{9,... | collective-permute-start | bytes 196616 | tf_op jit(solution)/shard_map/ppermute | solution.py:10
  6.4 1.2 dynamic_slice.9
  10.8 0.7 fusion.21
  11.5 1.2 dynamic_slice.10
  16.1 0.1 broadcast_and_fusion.1
  16.1 1.2 select_select_fusion.1
  17.4 1.5 collective-permute-start.1
  18.9 0.8 copy.93
  19.7 0.7 reshape.142
  20.4 1.3 fusion.25
  21.7 0.5 pad.2
  22.2 2.2 reshape.157
  24.3 0.0 copy-start.3
  24.4 0.0 copy-start.6
  24.4 12.6 %copy.92 = bf16[4,9,33,1,8,34]{4,0,5,2,1,3:T(4,128)(2,1)} copy(bf16[4,9,33,1,8,34]{5,4,2,1,0,3:T(8,128)(2,1)S(1)} %reshape.157) | data formatting | bytes 1292544 | tf_op jit(solution)/shard_map/conv_general_dilated | solution.py:55
  37.0 1.5 slice.19
  38.5 14.1 %broadcast_select_fusion = f32[4,16,8,17,32]{4,2,3,1,0:T(8,128)S(1)} fusion(pred[8,17]{0,1:T(8,128)(4,1)S(1)} %copy-done.6, bf16[4,9,33,1,7,2]{4,0,5,2,1,3:T(4,128)(2,1)S(1)} %slice.19, bf16[4,9,33,1,8,34]{4,0,5,2,1,3:T(4,128)(2,1)} %copy.92, bf16[32,4,3,3,3]{0,4,3,2,1:T(4,128)(2,1)S(1)} %copy-done.3), kind=kOutput, calls=%fused_computation.10 | convolution fusion | flops 62493440 | bytes 1800696 | tf_op jit(solution)/shard_map/conv_general_dilated | solution.py:55
  52.6 0.0 copy-start.5
  52.6 0.8 copy.95
  53.4 0.5 fusion.8
  53.9 3.6 %slice_bitcast_fusion.4 = (bf16[1,8,4,16,128]{1,3,4,2,0:T(8,128)(2,1)S(1)}, bf16[1,8,4,16,128]{1,3,4,2,0:T(8,128)(2,1)}, bf16[1,8,4,16,128]{1,3,4,2,0:T(8,128)(2,1)}, bf16[1,8,4,16,128]{1,3,4,2,0:T(8,128)(2,1)}) fusion(bf16[32,4,16,128]{0,2,3,1:T(8,128)(2,1)S(1)} %fusion.8), kind=kLoop, calls=%fused_computation.14 | loop fusion | bytes 1048576 | tf_op jit(solution)/shard_map/stack | solution.py:69
  57.6 3.0 %copy.99 = bf16[1,8,4,16,128]{4,3,2,1,0:T(8,128)(2,1)S(1)} copy(bf16[1,8,4,16,128]{1,3,4,2,0:T(8,128)(2,1)} %get-tuple-element.10) | data formatting | bytes 262144 | tf_op jit(solution)/shard_map/stack | solution.py:69
  60.5 0.0 copy-start.1
  60.5 3.6 %copy.98 = bf16[1,8,4,16,128]{4,3,2,1,0:T(8,128)(2,1)} copy(bf16[1,8,4,16,128]{1,3,4,2,0:T(8,128)(2,1)} %get-tuple-element.11) | data formatting | bytes 262144 | tf_op jit(solution)/shard_map/stack | solution.py:69
  64.2 3.6 %copy.97 = bf16[1,8,4,16,128]{4,3,2,1,0:T(8,128)(2,1)} copy(bf16[1,8,4,16,128]{1,3,4,2,0:T(8,128)(2,1)} %get-tuple-element.12) | data formatting | bytes 262144 | tf_op jit(solution)/shard_map/stack | solution.py:69
  67.7 2.4 copy.96
  70.1 1.9 pad_maximum_fusion
  72.0 4.9 %all-to-all-start = ((bf16[4,8,4,16,128]{4,3,2,1,0:T(8,128)(2,1)}), bf16[4,8,4,16,128]{4,3,2,1,0:T(8,128)(2,1)S(1)}, u32[]{:S(2)}, u32[]{:S(2)}) async-start(bf16[4,8,4,16,128]{4,3,2,1,0:T(8,128)(2,1)} %pad_maximum_fusion), calls=%async_computation | async-start | bytes 1048576 | tf_op jit(solution)/shard_map/all_to_all | solution.py:69
  76.9 0.1 iota_compare_fusion.1
  77.0 0.1 ge.51
  77.1 0.1 broadcast_and_fusion
  77.1 8.6 %all-to-all-done = bf16[4,8,4,16,128]{4,3,2,1,0:T(8,128)(2,1)S(1)} async-done(((bf16[4,8,4,16,128]{4,3,2,1,0:T(8,128)(2,1)}), bf16[4,8,4,16,128]{4,3,2,1,0:T(8,128)(2,1)S(1)}, u32[]{:S(2)}, u32[]{:S(2)}) %all-to-all-start) | async-done | bytes 524320 | tf_op jit(solution)/shard_map/all_to_all | solution.py:69
  85.7 1.3 fusion.19
  87.1 1.2 copy.101
  88.3 3.5 %all-to-all-start.1 = ((bf16[8,4,64,128]{3,1,0,2:T(4,128)(2,1)}), bf16[8,4,64,128]{3,1,0,2:T(4,128)(2,1)S(1)}, u32[]{:S(2)}, u32[]{:S(2)}) async-start(bf16[8,4,64,128]{3,1,0,2:T(4,128)(2,1)} %copy.101), calls=%async_computation.1 | async-start | bytes 1048576 | tf_op jit(solution)/shard_map/all_to_all | solution.py:78
  91.8 48.0 %copy.104 = bf16[4,1,9,33,256]{0,1,4,3,2:T(2,128)(2,1)} copy(bf16[4,1,9,33,256]{4,3,2,0,1:T(8,128)(2,1)S(1)} %copy-done) | data formatting | bytes 1216512 | tf_op jit(solution)/shard_map/broadcast_in_dim | solution.py:80
  139.7 0.2 copy.102
  140.0 0.2 convert_reduce_fusion
  140.2 0.1 copy.103
  140.2 0.1 copy.107
  140.3 0.7 broadcast_in_dim.115
  141.0 4.7 %copy.105 = bf16[32,1,4,16,128]{0,1,4,3,2:T(2,128)(2,1)} copy(bf16[32,1,4,16,128]{4,3,2,0,1:T(8,128)(2,1)S(1)} %bitcast.79) | data formatting | bytes 1048576 | tf_op jit(solution)/shard_map/broadcast_in_dim | solution.py:81
  145.7 87.7 %fusion.27 = f32[32,4,3,3,3]{0,1,4,3,2:T(4,128)S(1)} fusion(bf16[4,1,9,33,256]{0,1,4,3,2:T(2,128)(2,1)} %copy.104, bf16[32,1,4,16,128]{0,1,4,3,2:T(2,128)(2,1)} %copy.105), kind=kOutput, calls=%fused_computation.56 | convolution fusion | flops 56475648 | bytes 1146368 | tf_op jit(solution)/shard_map/transpose | solution.py:88
  233.5 0.1 copy.108
  233.5 0.1 pad_maximum_fusion.1
  233.6 41.0 %psum.7 = f32[32,109]{1,0:T(8,128)S(1)} all-reduce(f32[32,109]{1,0:T(8,128)S(1)} %pad_maximum_fusion.1), channel_id=1, replica_groups=mesh['gx'=8,'gy'=4] {'gx','gy'}, use_global_device_ids=true, to_apply=%region_1.2 | all-reduce | flops 3488 | bytes 27904 | tf_op jit(solution)/shard_map/psum | solution.py:91
  274.6 0.7 slice_reduce_fusion
  (23 shorter events, 0.2 us)
Async XLA Ops:
  1.5 14.7 %collective-permute-start = (bf16[4,32,256]{2,1,0:T(8,128)(2,1)S(1)}, bf16[4,32,256]{2,1,0:T(8,128)(2,1)S(1)}, u32[]{:S(2)}, u32[]{:S(2)}) collective-permute-start(bf16[4,32,256]{2,1,0:T(8,128)(2,1)S(1)} %slice_bitcast_fusion.5), channel_id=1, source_target_pairs={{0,4},{4,8},{8,12},{12,16},{16,20},{20,24},{24,28},{1,5},{5,9},{9,... | collective-permute-start | bytes 196616 | tf_op jit(solution)/shard_map/ppermute | solution.py:10
  17.4 3.0 %collective-permute-start.1 = (bf16[4,9,256]{2,0,1:T(4,128)(2,1)S(1)}, bf16[4,9,256]{2,0,1:T(4,128)(2,1)S(1)}, u32[]{:S(2)}, u32[]{:S(2)}) collective-permute-start(bf16[4,9,256]{2,0,1:T(4,128)(2,1)S(1)} %bitcast.80), channel_id=1, source_target_pairs={{0,1},{1,2},{2,3},{4,5},{5,6},{6,7},{8,9},{9,10},{10,11},{12,13},{... | collective-permute-start | bytes 55304 | tf_op jit(solution)/shard_map/ppermute | solution.py:10
  24.3 14.1 %copy-start.3 = (bf16[32,4,3,3,3]{0,4,3,2,1:T(4,128)(2,1)S(1)}, bf16[32,4,3,3,3]{0,4,3,2,1:T(4,128)(2,1)}, u32[]{:S(2)}) copy-start(bf16[32,4,3,3,3]{0,4,3,2,1:T(4,128)(2,1)} %reshape.142) | copy-start | bytes 20740
  24.4 14.1 %copy-start.6 = (pred[8,17]{0,1:T(8,128)(4,1)S(1)}, pred[8,17]{0,1:T(8,128)(4,1)}, u32[]{:S(2)}) copy-start(pred[8,17]{0,1:T(8,128)(4,1)} %constant.67) | copy-start | bytes 412
  52.6 0.8 copy-start.5
  60.5 25.2 %copy-start.1 = (bf16[8,4,64,128]{3,2,1,0:T(8,128)(2,1)S(1)}, bf16[8,4,64,128]{3,2,1,0:T(8,128)(2,1)}, u32[]{:S(2)}) copy-start(bf16[8,4,64,128]{3,2,1,0:T(8,128)(2,1)} %param.11) | copy-start | bytes 1572868
  67.7 24.0 %copy-start = (bf16[4,1,9,33,256]{4,3,2,0,1:T(8,128)(2,1)S(1)}, bf16[4,1,9,33,256]{4,3,2,0,1:T(8,128)(2,1)}, u32[]{:S(2)}) copy-start(bf16[4,1,9,33,256]{4,3,2,0,1:T(8,128)(2,1)} %get-tuple-element.13) | copy-start | bytes 1824772
  72.0 13.7 %all-to-all-start = ((bf16[4,8,4,16,128]{4,3,2,1,0:T(8,128)(2,1)}), bf16[4,8,4,16,128]{4,3,2,1,0:T(8,128)(2,1)S(1)}, u32[]{:S(2)}, u32[]{:S(2)}) async-start(bf16[4,8,4,16,128]{4,3,2,1,0:T(8,128)(2,1)} %pad_maximum_fusion), calls=%async_computation | async-start | bytes 1048576 | tf_op jit(solution)/shard_map/all_to_all | solution.py:69
  88.3 51.5 %all-to-all-start.1 = ((bf16[8,4,64,128]{3,1,0,2:T(4,128)(2,1)}), bf16[8,4,64,128]{3,1,0,2:T(4,128)(2,1)S(1)}, u32[]{:S(2)}, u32[]{:S(2)}) async-start(bf16[8,4,64,128]{3,1,0,2:T(4,128)(2,1)} %copy.101), calls=%async_computation.1 | async-start | bytes 1048576 | tf_op jit(solution)/shard_map/all_to_all | solution.py:78
  145.7 87.8 %copy-start.2 = (f32[32,1]{1,0:T(8,128)S(1)}, f32[32,1]{1,0:T(8,128)}, u32[]{:S(2)}) copy-start(f32[32,1]{1,0:T(8,128)} %broadcast_in_dim.115) | copy-start | bytes 388
  274.6 0.7 copy-start.4
